TPU v7x, 128 devices: a whole 4x4x4 slice. The times are simulated.
128 devices in a mesh: row: 4 (over z_hi, core), circ: 32 (over x, y, z_lo).
Axes of the slice: x: 4, y: 4, z: 4 (z_hi: 2, z_lo: 2; z = z_hi * 2 + z_lo), core: 2. Of those that a mesh axis runs over, the one named last changes fastest.
Arguments:
- flow_state: float32 [5, 64, 32, 4096], P(None, 'row', None, 'circ'), may hold values from -4 to 4
- velocity: float32 [3, 64, 32, 4096], P(None, 'row', None, 'circ'), may hold values from -3 to 3
- offsets: int32 [3, 3], replicated, may hold values from 0 to 4095, as said below
- passage_shift: int32 [4], replicated, may hold values from 0 to 31, as said below
- donor_step: int32 [4, 2, 4096], P('row', None, 'circ'), may hold values from 0 to 127
- donor_weight: float32 [4, 2, 4096], P('row', None, 'circ'), may hold values from 0.05 to 0.95
Outputs:
- updated_state: float32 [5, 64, 32, 4096], P(None, 'row', None, 'circ')
Inputs may be any that keep to these rules, and one draw needn't show every extreme that they name: Rotation offsets in cells; some interface takes the offset 4096 - 1 at some section in every draw, and with two or more interfaces some takes 0. `passage_shift`: passage index placed on device column 0 of each row; some row has 32 - 1 and some row 0 in every draw.
All inputs are finite; a program needn't handle non-finite values.
Results may differ from a plain program's by a relative error of at most 0.0003.
Values sent between devices are 32-bit elements; how exact they have to be, the bound alone decides.
No kernel may reach another device: no remote copies, remote signals or barrier semaphores. Data moves between devices by JAX's collectives and lax.ppermute only.
A program may use at most 128 MiB of HBM per device.

v0:
```python
import jax
import jax.numpy as jnp
from jax import lax
from jax.sharding import PartitionSpec as P


SMAG_COEF = 0.1
TIME_STEP = 0.25
RADICES = (8, 4)


def extended(cells, sides, width):
    for axis, dim in sides:
        count = lax.axis_size(axis)
        head = lax.slice_in_dim(cells, 0, width, axis=dim)
        tail = lax.slice_in_dim(cells, cells.shape[dim] - width, cells.shape[dim], axis=dim)
        cells = jnp.concatenate(
            [
                lax.ppermute(tail, axis, [(i, (i + 1) % count) for i in range(count)]),
                cells,
                lax.ppermute(head, axis, [((i + 1) % count, i) for i in range(count)]),
            ],
            axis=dim,
        )
    return cells


def combine(fields, axial_ext, radial_ext, around_ext, velocity):
    d_axial = 0.5 * (axial_ext[:, 2:] - axial_ext[:, :-2])
    d_radial = 0.5 * (radial_ext[:, :, 2:] - radial_ext[:, :, :-2])
    d_around = 0.5 * (around_ext[..., 2:] - around_ext[..., :-2])
    laplace = (
        axial_ext[:, 2:]
        + axial_ext[:, :-2]
        + radial_ext[:, :, 2:]
        + radial_ext[:, :, :-2]
        + around_ext[..., 2:]
        + around_ext[..., :-2]
        - 6.0 * fields
    )
    strain = jnp.sum(d_axial[1:4] ** 2 + d_radial[1:4] ** 2 + d_around[1:4] ** 2, axis=0)
    eddy_visc = SMAG_COEF * jnp.sqrt(strain + 1.0)
    return eddy_visc * laplace - (
        velocity[0] * d_axial + velocity[1] * d_radial + velocity[2] * d_around
    )


def radial_pad(fields):
    return jnp.concatenate([fields[:, :, :1], fields, fields[:, :, -1:]], axis=2)


def axial_pad(fields, lower_ghost, upper_ghost):
    return jnp.concatenate([lower_ghost[:, None], fields, upper_ghost[:, None]], axis=1)


def local(flow_state, velocity, offsets, passage_shift, donor_step, donor_weight):
    row_count = lax.axis_size("row")
    loop_size = lax.axis_size("circ")
    row_id = lax.axis_index("row")
    pitch_cells = flow_state.shape[-1]
    loop_cells = pitch_cells * loop_size
    lower_src = jnp.maximum(row_id - 1, 0)
    upper_src = jnp.minimum(row_id + 1, row_count - 1)
    lower_face = jnp.maximum(row_id - 1, 0)
    upper_face = jnp.minimum(row_id, row_count - 2)
    window = 3 * pitch_cells

    def from_row(plane, step, shift):
        pairs = []
        for r in range(row_count):
            src = r + step
            if 0 <= src < row_count:
                for b in range(loop_size):
                    pairs.append((src * loop_size + (b + shift) % loop_size, r * loop_size + b))
        return lax.ppermute(plane, ("row", "circ"), pairs)

    def along_circ(value, shift):
        return lax.ppermute(
            value, "circ", [((b + shift) % loop_size, b) for b in range(loop_size)]
        )

    def picks(section_index):
        low_offset = offsets[section_index, lower_face]
        high_offset = (loop_cells - offsets[section_index, upper_face]) % loop_cells
        offs = jnp.stack([low_offset, high_offset])
        coarse = offs // pitch_cells
        fine = offs % pitch_cells
        sources = jnp.stack([lower_src, upper_src])
        dq = (coarse + passage_shift[sources] - passage_shift[row_id]) % loop_size
        first_col = (
            jnp.arange(pitch_cells, dtype=jnp.int32)[None, :] + fine[:, None] + donor_step[0]
        )
        weights = donor_weight[0]
        rows = jnp.arange(window, dtype=jnp.int32)[None, :, None]
        pick = jnp.where(rows == first_col[:, None, :], weights[:, None, :], 0.0) + jnp.where(
            rows == first_col[:, None, :] + 1, 1.0 - weights[:, None, :], 0.0
        )
        return dq, pick.reshape(2, 3, pitch_cells, pitch_cells)

    def ghosts(last_plane, first_plane, section_index):
        dq, pick = picks(section_index)
        first = RADICES[0]
        digit = dq % first
        blocks = []
        for d, (plane, step) in enumerate(((last_plane, -1), (first_plane, 1))):
            got = [from_row(plane, step, j) for j in range(first + 2)]
            blocks.append(jnp.stack([lax.select_n(digit[d], *got[i : i + first]) for i in range(3)]))
        stack = jnp.stack(blocks)
        span = first
        rest = dq // first
        for radix in RADICES[1:]:
            digit = rest % radix
            rest = rest // radix
            got = [stack] + [along_circ(stack, span * c) for c in range(1, radix)]
            stack = jnp.stack([lax.select_n(digit[d], *[g[d] for g in got]) for d in range(2)])
            span *= radix
        comps, radial = last_plane.shape[0], last_plane.shape[1]
        win = stack.reshape(2, 3, comps * radial, pitch_cells)
        out = [
            sum(
                jnp.dot(win[d, i], pick[d, i], precision=lax.Precision.HIGHEST) for i in range(3)
            ).reshape(comps, radial, pitch_cells)
            for d in range(2)
        ]
        return out[0], out[1]

    def evaluate_section(fields, section_index):
        first_plane = fields[:, 0]
        last_plane = fields[:, -1]
        around_ext = extended(fields, (("circ", 3),), 1)
        lower_ghost, upper_ghost = ghosts(last_plane, first_plane, section_index)
        lower_ghost = jnp.where(row_id == 0, first_plane, lower_ghost)
        upper_ghost = jnp.where(row_id == row_count - 1, last_plane, upper_ghost)
        return combine(
            fields,
            axial_pad(fields, lower_ghost, upper_ghost),
            radial_pad(fields),
            around_ext,
            velocity,
        )

    section_one = flow_state + TIME_STEP * evaluate_section(flow_state, 0)
    section_two = 0.75 * flow_state + 0.25 * (section_one + TIME_STEP * evaluate_section(section_one, 1))
    return 1.0 / 3.0 * flow_state + 2.0 / 3.0 * (section_two + TIME_STEP * evaluate_section(section_two, 2))


def solution(mesh):
    placed = (
        P(None, "row", None, "circ"),
        P(None, "row", None, "circ"),
        P(),
        P(),
        P("row", None, "circ"),
        P("row", None, "circ"),
    )
    return jax.shard_map(
        local, mesh=mesh, in_specs=placed, out_specs=P(None, "row", None, "circ"), check_vma=False
    )
```

profile of v0, /device:TPU:1, one launch (start us, length us, event | category | flops | bytes accessed | tf_op | source)
XLA Modules:
  0.0 349.3 jit_solution(15996221815683321619)
XLA Ops:
  1.6 6.9 %collective-permute-start.10 = (f32[5,32,128]{2,1,0:T(8,128)}, f32[5,32,128]{2,1,0:T(8,128)S(1)}, u32[]{:S(2)}, u32[]{:S(2)}) collective-permute-start(f32[5,32,128]{2,1,0:T(8,128)} %get-tuple-element.58), channel_id=1, source_target_pairs={{0,32},{1,33},{2,34},{3,35},{4,36},{5,37},{6,38},{7,39},{8,40},{9,... | collective-permute-start | bytes 245768 | tf_op jit(solution)/shard_map/ppermute | solution.py:75
  8.5 6.7 %collective-permute-start.11 = (f32[5,32,128]{2,1,0:T(8,128)}, f32[5,32,128]{2,1,0:T(8,128)}, u32[]{:S(2)}, u32[]{:S(2)}) collective-permute-start(f32[5,32,128]{2,1,0:T(8,128)} %get-tuple-element.58), channel_id=1, source_target_pairs={{1,32},{2,33},{3,34},{4,35},{5,36},{6,37},{7,38},{8,39},{9,40},{10... | collective-permute-start | bytes 245768 | tf_op jit(solution)/shard_map/ppermute | solution.py:75
  24.9 3.5 %fusion.50 = (f32[5,16,32,1]{3,2,1,0:T(8,128)S(1)}, f32[5,16,32,1]{3,2,1,0:T(8,128)}) fusion(f32[5,16,32,128]{3,2,1,0:T(8,128)} %param.6), kind=kLoop, calls=%fused_computation.256 | loop fusion | bytes 40960 | tf_op jit(solution)/shard_map/slice | solution.py:16
  32.9 3.0 and_select_fusion.2
  57.8 2.5 copy.94
  61.4 4.8 %collective-permute-start = (f32[5,32,128]{2,1,0:T(8,128)}, f32[5,32,128]{2,1,0:T(8,128)S(1)}, u32[]{:S(2)}, u32[]{:S(2)}) collective-permute-start(f32[5,32,128]{2,1,0:T(8,128)} %get-tuple-element.59), channel_id=1, source_target_pairs={{32,0},{33,1},{34,2},{35,3},{36,4},{37,5},{38,6},{39,7},{40,8},{41... | collective-permute-start | bytes 245768 | tf_op jit(solution)/shard_map/ppermute | solution.py:75
  66.2 3.8 %collective-permute-start.1 = (f32[5,32,128]{2,1,0:T(8,128)}, f32[5,32,128]{2,1,0:T(8,128)S(1)}, u32[]{:S(2)}, u32[]{:S(2)}) collective-permute-start(f32[5,32,128]{2,1,0:T(8,128)} %get-tuple-element.59), channel_id=1, source_target_pairs={{33,0},{34,1},{35,2},{36,3},{37,4},{38,5},{39,6},{40,7},{41,8},{42... | collective-permute-start | bytes 245768 | tf_op jit(solution)/shard_map/ppermute | solution.py:75
  87.0 2.7 collective-permute-start.23
  109.6 6.0 %collective-permute-done.20 = f32[2,3,5,32,128]{4,3,2,1,0:T(8,128)} collective-permute-done((f32[2,3,5,32,128]{4,3,2,1,0:T(8,128)}, f32[2,3,5,32,128]{4,3,2,1,0:T(8,128)}, u32[]{:S(2)}, u32[]{:S(2)}) %collective-permute-start.20) | collective-permute-done | bytes 491552 | tf_op jit(solution)/shard_map/ppermute | solution.py:78
  115.5 3.6 %collective-permute-done.22 = f32[2,3,5,32,128]{4,3,2,1,0:T(8,128)} collective-permute-done((f32[2,3,5,32,128]{4,3,2,1,0:T(8,128)}, f32[2,3,5,32,128]{4,3,2,1,0:T(8,128)}, u32[]{:S(2)}, u32[]{:S(2)}) %collective-permute-start.22) | collective-permute-done | bytes 491552 | tf_op jit(solution)/shard_map/ppermute | solution.py:78
  127.6 7.5 %collective-permute-start.35 = (f32[5,32,128]{2,1,0:T(8,128)S(1)}, f32[5,32,128]{2,1,0:T(8,128)S(1)}, u32[]{:S(2)}, u32[]{:S(2)}) collective-permute-start(f32[5,32,128]{2,1,0:T(8,128)S(1)} %get-tuple-element.47), channel_id=1, source_target_pairs={{0,32},{1,33},{2,34},{3,35},{4,36},{5,37},{6,38},{7,39},{8,40},{9,... | collective-permute-start | bytes 245768 | tf_op jit(solution)/shard_map/ppermute | solution.py:75
  135.1 4.0 %collective-permute-start.36 = (f32[5,32,128]{2,1,0:T(8,128)S(1)}, f32[5,32,128]{2,1,0:T(8,128)S(1)}, u32[]{:S(2)}, u32[]{:S(2)}) collective-permute-start(f32[5,32,128]{2,1,0:T(8,128)S(1)} %get-tuple-element.47), channel_id=1, source_target_pairs={{1,32},{2,33},{3,34},{4,35},{5,36},{6,37},{7,38},{8,39},{9,40},{10... | collective-permute-start | bytes 245768 | tf_op jit(solution)/shard_map/ppermute | solution.py:75
  160.5 2.5 collective-permute-start.43
  169.2 3.1 collective-permute-start.25
  172.3 3.0 collective-permute-start.26
  189.3 2.7 collective-permute-start.34
  194.7 2.5 collective-permute-done.33
  199.7 4.4 %collective-permute-start.45 = (f32[2,3,5,32,128]{4,3,2,1,0:T(8,128)}, f32[2,3,5,32,128]{4,3,2,1,0:T(8,128)}, u32[]{:S(2)}, u32[]{:S(2)}) collective-permute-start(f32[2,3,5,32,128]{4,3,2,1,0:T(8,128)} %pad_maximum_fusion.19), channel_id=1, source_target_pairs={{8,0},{9,1},{10,2},{11,3},{12,4},{13,5},{14,6},{15,7},{16,8},{17,9... | collective-permute-start | bytes 1474568 | tf_op jit(solution)/shard_map/ppermute | solution.py:78
  206.7 2.5 copy.85
  209.2 4.5 %collective-permute-start.48 = (f32[5,16,32,1]{2,1,3,0:T(8,128)}, f32[5,16,32,1]{2,1,3,0:T(8,128)}, u32[]{:S(2)}, u32[]{:S(2)}) collective-permute-start(f32[5,16,32,1]{2,1,3,0:T(8,128)} %copy.85), channel_id=1, source_target_pairs={{1,0},{2,1},{3,2},{4,3},{5,4},{6,5},{7,6},{8,7},{9,8},{10,9},{11,1... | collective-permute-start | bytes 30728 | tf_op jit(solution)/shard_map/ppermute | solution.py:21
  213.7 2.5 copy.87
  216.8 4.7 %collective-permute-done.48 = f32[5,16,32,1]{2,1,3,0:T(8,128)} collective-permute-done((f32[5,16,32,1]{2,1,3,0:T(8,128)}, f32[5,16,32,1]{2,1,3,0:T(8,128)}, u32[]{:S(2)}, u32[]{:S(2)}) %collective-permute-start.48) | collective-permute-done | bytes 10272 | tf_op jit(solution)/shard_map/ppermute | solution.py:21
  223.9 5.6 %collective-permute-done.49 = f32[5,16,32,1]{2,1,3,0:T(8,128)} collective-permute-done((f32[5,16,32,1]{2,1,3,0:T(8,128)}, f32[5,16,32,1]{2,1,3,0:T(8,128)}, u32[]{:S(2)}, u32[]{:S(2)}) %collective-permute-start.49) | collective-permute-done | bytes 10272 | tf_op jit(solution)/shard_map/ppermute | solution.py:19
  242.7 6.5 %collective-permute-start.61 = (f32[5,32,128]{2,1,0:T(8,128)S(1)}, f32[5,32,128]{2,1,0:T(8,128)S(1)}, u32[]{:S(2)}, u32[]{:S(2)}) collective-permute-start(f32[5,32,128]{2,1,0:T(8,128)S(1)} %get-tuple-element.36), channel_id=1, source_target_pairs={{1,32},{2,33},{3,34},{4,35},{5,36},{6,37},{7,38},{8,39},{9,40},{10... | collective-permute-start | bytes 245768 | tf_op jit(solution)/shard_map/ppermute | solution.py:75
  279.3 4.3 %collective-permute-start.50 = (f32[5,32,128]{2,1,0:T(8,128)S(1)}, f32[5,32,128]{2,1,0:T(8,128)S(1)}, u32[]{:S(2)}, u32[]{:S(2)}) collective-permute-start(f32[5,32,128]{2,1,0:T(8,128)S(1)} %get-tuple-element.37), channel_id=1, source_target_pairs={{32,0},{33,1},{34,2},{35,3},{36,4},{37,5},{38,6},{39,7},{40,8},{41... | collective-permute-start | bytes 245768 | tf_op jit(solution)/shard_map/ppermute | solution.py:75
  283.7 3.0 collective-permute-start.51
  304.6 2.5 collective-permute-done.57
  314.7 2.5 copy.89
  317.2 5.6 %collective-permute-start.73 = (f32[5,16,32,1]{2,1,3,0:T(8,128)}, f32[5,16,32,1]{2,1,3,0:T(8,128)}, u32[]{:S(2)}, u32[]{:S(2)}) collective-permute-start(f32[5,16,32,1]{2,1,3,0:T(8,128)} %copy.89), channel_id=1, source_target_pairs={{1,0},{2,1},{3,2},{4,3},{5,4},{6,5},{7,6},{8,7},{9,8},{10,9},{11,1... | collective-permute-start | bytes 30728 | tf_op jit(solution)/shard_map/ppermute | solution.py:21
  322.8 2.5 copy.91
  325.9 5.6 %collective-permute-done.73 = f32[5,16,32,1]{2,1,3,0:T(8,128)} collective-permute-done((f32[5,16,32,1]{2,1,3,0:T(8,128)}, f32[5,16,32,1]{2,1,3,0:T(8,128)}, u32[]{:S(2)}, u32[]{:S(2)}) %collective-permute-start.73) | collective-permute-done | bytes 10272 | tf_op jit(solution)/shard_map/ppermute | solution.py:21
  333.9 4.4 %collective-permute-done.74 = f32[5,16,32,1]{2,1,3,0:T(8,128)} collective-permute-done((f32[5,16,32,1]{2,1,3,0:T(8,128)}, f32[5,16,32,1]{2,1,3,0:T(8,128)}, u32[]{:S(2)}, u32[]{:S(2)}) %collective-permute-start.74) | collective-permute-done | bytes 10272 | tf_op jit(solution)/shard_map/ppermute | solution.py:19
  (302 shorter events, 177.5 us)
Async XLA Ops:
  1.6 37.4 %collective-permute-start.10 = (f32[5,32,128]{2,1,0:T(8,128)}, f32[5,32,128]{2,1,0:T(8,128)S(1)}, u32[]{:S(2)}, u32[]{:S(2)}) collective-permute-start(f32[5,32,128]{2,1,0:T(8,128)} %get-tuple-element.58), channel_id=1, source_target_pairs={{0,32},{1,33},{2,34},{3,35},{4,36},{5,37},{6,38},{7,39},{8,40},{9,... | collective-permute-start | bytes 245768 | tf_op jit(solution)/shard_map/ppermute | solution.py:75
  8.5 32.5 %collective-permute-start.11 = (f32[5,32,128]{2,1,0:T(8,128)}, f32[5,32,128]{2,1,0:T(8,128)}, u32[]{:S(2)}, u32[]{:S(2)}) collective-permute-start(f32[5,32,128]{2,1,0:T(8,128)} %get-tuple-element.58), channel_id=1, source_target_pairs={{1,32},{2,33},{3,34},{4,35},{5,36},{6,37},{7,38},{8,39},{9,40},{10... | collective-permute-start | bytes 245768 | tf_op jit(solution)/shard_map/ppermute | solution.py:75
  15.2 27.7 %collective-permute-start.12 = (f32[5,32,128]{2,1,0:T(8,128)}, f32[5,32,128]{2,1,0:T(8,128)}, u32[]{:S(2)}, u32[]{:S(2)}) collective-permute-start(f32[5,32,128]{2,1,0:T(8,128)} %get-tuple-element.58), channel_id=1, source_target_pairs={{2,32},{3,33},{4,34},{5,35},{6,36},{7,37},{8,38},{9,39},{10,40},{1... | collective-permute-start | bytes 245768 | tf_op jit(solution)/shard_map/ppermute | solution.py:75
  17.6 27.3 %collective-permute-start.13 = (f32[5,32,128]{2,1,0:T(8,128)}, f32[5,32,128]{2,1,0:T(8,128)}, u32[]{:S(2)}, u32[]{:S(2)}) collective-permute-start(f32[5,32,128]{2,1,0:T(8,128)} %get-tuple-element.58), channel_id=1, source_target_pairs={{3,32},{4,33},{5,34},{6,35},{7,36},{8,37},{9,38},{10,39},{11,40},{... | collective-permute-start | bytes 245768 | tf_op jit(solution)/shard_map/ppermute | solution.py:75
  19.5 27.3 %collective-permute-start.14 = (f32[5,32,128]{2,1,0:T(8,128)}, f32[5,32,128]{2,1,0:T(8,128)}, u32[]{:S(2)}, u32[]{:S(2)}) collective-permute-start(f32[5,32,128]{2,1,0:T(8,128)} %get-tuple-element.58), channel_id=1, source_target_pairs={{4,32},{5,33},{6,34},{7,35},{8,36},{9,37},{10,38},{11,39},{12,40},... | collective-permute-start | bytes 245768 | tf_op jit(solution)/shard_map/ppermute | solution.py:75
  39.0 22.4 %collective-permute-start.15 = (f32[5,32,128]{2,1,0:T(8,128)}, f32[5,32,128]{2,1,0:T(8,128)}, u32[]{:S(2)}, u32[]{:S(2)}) collective-permute-start(f32[5,32,128]{2,1,0:T(8,128)} %get-tuple-element.58), channel_id=1, source_target_pairs={{5,32},{6,33},{7,34},{8,35},{9,36},{10,37},{11,38},{12,39},{13,40}... | collective-permute-start | bytes 245768 | tf_op jit(solution)/shard_map/ppermute | solution.py:75
  41.0 25.3 %collective-permute-start.16 = (f32[5,32,128]{2,1,0:T(8,128)}, f32[5,32,128]{2,1,0:T(8,128)}, u32[]{:S(2)}, u32[]{:S(2)}) collective-permute-start(f32[5,32,128]{2,1,0:T(8,128)} %get-tuple-element.58), channel_id=1, source_target_pairs={{6,32},{7,33},{8,34},{9,35},{10,36},{11,37},{12,38},{13,39},{14,40... | collective-permute-start | bytes 245768 | tf_op jit(solution)/shard_map/ppermute | solution.py:75
  42.9 27.2 %collective-permute-start.17 = (f32[5,32,128]{2,1,0:T(8,128)}, f32[5,32,128]{2,1,0:T(8,128)}, u32[]{:S(2)}, u32[]{:S(2)}) collective-permute-start(f32[5,32,128]{2,1,0:T(8,128)} %get-tuple-element.58), channel_id=1, source_target_pairs={{7,32},{8,33},{9,34},{10,35},{11,36},{12,37},{13,38},{14,39},{15,4... | collective-permute-start | bytes 245768 | tf_op jit(solution)/shard_map/ppermute | solution.py:75
  44.8 27.2 %collective-permute-start.18 = (f32[5,32,128]{2,1,0:T(8,128)}, f32[5,32,128]{2,1,0:T(8,128)}, u32[]{:S(2)}, u32[]{:S(2)}) collective-permute-start(f32[5,32,128]{2,1,0:T(8,128)} %get-tuple-element.58), channel_id=1, source_target_pairs={{8,32},{9,33},{10,34},{11,35},{12,36},{13,37},{14,38},{15,39},{16,... | collective-permute-start | bytes 245768 | tf_op jit(solution)/shard_map/ppermute | solution.py:75
  46.9 27.1 %collective-permute-start.19 = (f32[5,32,128]{2,1,0:T(8,128)}, f32[5,32,128]{2,1,0:T(8,128)}, u32[]{:S(2)}, u32[]{:S(2)}) collective-permute-start(f32[5,32,128]{2,1,0:T(8,128)} %get-tuple-element.58), channel_id=1, source_target_pairs={{9,32},{10,33},{11,34},{12,35},{13,36},{14,37},{15,38},{16,39},{17... | collective-permute-start | bytes 245768 | tf_op jit(solution)/shard_map/ppermute | solution.py:75
  87.0 18.8 %collective-permute-start.23 = (f32[5,16,32,1]{2,1,3,0:T(8,128)S(1)}, f32[5,16,32,1]{2,1,3,0:T(8,128)}, u32[]{:S(2)}, u32[]{:S(2)}) collective-permute-start(f32[5,16,32,1]{2,1,3,0:T(8,128)S(1)} %copy-done.34), channel_id=1, source_target_pairs={{1,0},{2,1},{3,2},{4,3},{5,4},{6,5},{7,6},{8,7},{9,8},{10,9},{11,1... | collective-permute-start | bytes 30728 | tf_op jit(solution)/shard_map/ppermute | solution.py:21
  95.4 20.1 %collective-permute-start.20 = (f32[2,3,5,32,128]{4,3,2,1,0:T(8,128)}, f32[2,3,5,32,128]{4,3,2,1,0:T(8,128)}, u32[]{:S(2)}, u32[]{:S(2)}) collective-permute-start(f32[2,3,5,32,128]{4,3,2,1,0:T(8,128)} %pad_maximum_fusion.18), channel_id=1, source_target_pairs={{8,0},{9,1},{10,2},{11,3},{12,4},{13,5},{14,6},{15,7},{16,8},{17,9... | collective-permute-start | bytes 1474568 | tf_op jit(solution)/shard_map/ppermute | solution.py:78
  96.5 19.1 %collective-permute-start.21 = (f32[2,3,5,32,128]{4,3,2,1,0:T(8,128)}, f32[2,3,5,32,128]{4,3,2,1,0:T(8,128)}, u32[]{:S(2)}, u32[]{:S(2)}) collective-permute-start(f32[2,3,5,32,128]{4,3,2,1,0:T(8,128)} %pad_maximum_fusion.18), channel_id=1, source_target_pairs={{16,0},{17,1},{18,2},{19,3},{20,4},{21,5},{22,6},{23,7},{24,8},{25... | collective-permute-start | bytes 1474568 | tf_op jit(solution)/shard_map/ppermute | solution.py:78
  98.1 21.0 %collective-permute-start.22 = (f32[2,3,5,32,128]{4,3,2,1,0:T(8,128)}, f32[2,3,5,32,128]{4,3,2,1,0:T(8,128)}, u32[]{:S(2)}, u32[]{:S(2)}) collective-permute-start(f32[2,3,5,32,128]{4,3,2,1,0:T(8,128)} %pad_maximum_fusion.18), channel_id=1, source_target_pairs={{24,0},{25,1},{26,2},{27,3},{28,4},{29,5},{30,6},{31,7},{0,8},{1,9... | collective-permute-start | bytes 1474568 | tf_op jit(solution)/shard_map/ppermute | solution.py:78
  127.6 27.1 %collective-permute-start.35 = (f32[5,32,128]{2,1,0:T(8,128)S(1)}, f32[5,32,128]{2,1,0:T(8,128)S(1)}, u32[]{:S(2)}, u32[]{:S(2)}) collective-permute-start(f32[5,32,128]{2,1,0:T(8,128)S(1)} %get-tuple-element.47), channel_id=1, source_target_pairs={{0,32},{1,33},{2,34},{3,35},{4,36},{5,37},{6,38},{7,39},{8,40},{9,... | collective-permute-start | bytes 245768 | tf_op jit(solution)/shard_map/ppermute | solution.py:75
  135.1 21.4 %collective-permute-start.36 = (f32[5,32,128]{2,1,0:T(8,128)S(1)}, f32[5,32,128]{2,1,0:T(8,128)S(1)}, u32[]{:S(2)}, u32[]{:S(2)}) collective-permute-start(f32[5,32,128]{2,1,0:T(8,128)S(1)} %get-tuple-element.47), channel_id=1, source_target_pairs={{1,32},{2,33},{3,34},{4,35},{5,36},{6,37},{7,38},{8,39},{9,40},{10... | collective-permute-start | bytes 245768 | tf_op jit(solution)/shard_map/ppermute | solution.py:75
  139.2 19.3 %collective-permute-start.37 = (f32[5,32,128]{2,1,0:T(8,128)S(1)}, f32[5,32,128]{2,1,0:T(8,128)S(1)}, u32[]{:S(2)}, u32[]{:S(2)}) collective-permute-start(f32[5,32,128]{2,1,0:T(8,128)S(1)} %get-tuple-element.47), channel_id=1, source_target_pairs={{2,32},{3,33},{4,34},{5,35},{6,36},{7,37},{8,38},{9,39},{10,40},{1... | collective-permute-start | bytes 245768 | tf_op jit(solution)/shard_map/ppermute | solution.py:75
  141.1 19.3 %collective-permute-start.38 = (f32[5,32,128]{2,1,0:T(8,128)S(1)}, f32[5,32,128]{2,1,0:T(8,128)S(1)}, u32[]{:S(2)}, u32[]{:S(2)}) collective-permute-start(f32[5,32,128]{2,1,0:T(8,128)S(1)} %get-tuple-element.47), channel_id=1, source_target_pairs={{3,32},{4,33},{5,34},{6,35},{7,36},{8,37},{9,38},{10,39},{11,40},{... | collective-permute-start | bytes 245768 | tf_op jit(solution)/shard_map/ppermute | solution.py:75
  143.0 19.9 %collective-permute-start.39 = (f32[5,32,128]{2,1,0:T(8,128)S(1)}, f32[5,32,128]{2,1,0:T(8,128)S(1)}, u32[]{:S(2)}, u32[]{:S(2)}) collective-permute-start(f32[5,32,128]{2,1,0:T(8,128)S(1)} %get-tuple-element.47), channel_id=1, source_target_pairs={{4,32},{5,33},{6,34},{7,35},{8,36},{9,37},{10,38},{11,39},{12,40},... | collective-permute-start | bytes 245768 | tf_op jit(solution)/shard_map/ppermute | solution.py:75
  199.7 32.2 %collective-permute-start.45 = (f32[2,3,5,32,128]{4,3,2,1,0:T(8,128)}, f32[2,3,5,32,128]{4,3,2,1,0:T(8,128)}, u32[]{:S(2)}, u32[]{:S(2)}) collective-permute-start(f32[2,3,5,32,128]{4,3,2,1,0:T(8,128)} %pad_maximum_fusion.19), channel_id=1, source_target_pairs={{8,0},{9,1},{10,2},{11,3},{12,4},{13,5},{14,6},{15,7},{16,8},{17,9... | collective-permute-start | bytes 1474568 | tf_op jit(solution)/shard_map/ppermute | solution.py:78
  204.1 27.9 %collective-permute-start.46 = (f32[2,3,5,32,128]{4,3,2,1,0:T(8,128)}, f32[2,3,5,32,128]{4,3,2,1,0:T(8,128)}, u32[]{:S(2)}, u32[]{:S(2)}) collective-permute-start(f32[2,3,5,32,128]{4,3,2,1,0:T(8,128)} %pad_maximum_fusion.19), channel_id=1, source_target_pairs={{16,0},{17,1},{18,2},{19,3},{20,4},{21,5},{22,6},{23,7},{24,8},{25... | collective-permute-start | bytes 1474568 | tf_op jit(solution)/shard_map/ppermute | solution.py:78
  204.1 27.9 %collective-permute-start.47 = (f32[2,3,5,32,128]{4,3,2,1,0:T(8,128)}, f32[2,3,5,32,128]{4,3,2,1,0:T(8,128)}, u32[]{:S(2)}, u32[]{:S(2)}) collective-permute-start(f32[2,3,5,32,128]{4,3,2,1,0:T(8,128)} %pad_maximum_fusion.19), channel_id=1, source_target_pairs={{24,0},{25,1},{26,2},{27,3},{28,4},{29,5},{30,6},{31,7},{0,8},{1,9... | collective-permute-start | bytes 1474568 | tf_op jit(solution)/shard_map/ppermute | solution.py:78
  240.3 24.8 %collective-permute-start.60 = (f32[5,32,128]{2,1,0:T(8,128)S(1)}, f32[5,32,128]{2,1,0:T(8,128)S(1)}, u32[]{:S(2)}, u32[]{:S(2)}) collective-permute-start(f32[5,32,128]{2,1,0:T(8,128)S(1)} %get-tuple-element.36), channel_id=1, source_target_pairs={{0,32},{1,33},{2,34},{3,35},{4,36},{5,37},{6,38},{7,39},{8,40},{9,... | collective-permute-start | bytes 245768 | tf_op jit(solution)/shard_map/ppermute | solution.py:75
  242.7 24.3 %collective-permute-start.61 = (f32[5,32,128]{2,1,0:T(8,128)S(1)}, f32[5,32,128]{2,1,0:T(8,128)S(1)}, u32[]{:S(2)}, u32[]{:S(2)}) collective-permute-start(f32[5,32,128]{2,1,0:T(8,128)S(1)} %get-tuple-element.36), channel_id=1, source_target_pairs={{1,32},{2,33},{3,34},{4,35},{5,36},{6,37},{7,38},{8,39},{9,40},{10... | collective-permute-start | bytes 245768 | tf_op jit(solution)/shard_map/ppermute | solution.py:75
  249.3 19.7 %collective-permute-start.62 = (f32[5,32,128]{2,1,0:T(8,128)S(1)}, f32[5,32,128]{2,1,0:T(8,128)S(1)}, u32[]{:S(2)}, u32[]{:S(2)}) collective-permute-start(f32[5,32,128]{2,1,0:T(8,128)S(1)} %get-tuple-element.36), channel_id=1, source_target_pairs={{2,32},{3,33},{4,34},{5,35},{6,36},{7,37},{8,38},{9,39},{10,40},{1... | collective-permute-start | bytes 245768 | tf_op jit(solution)/shard_map/ppermute | solution.py:75
  251.2 19.7 %collective-permute-start.63 = (f32[5,32,128]{2,1,0:T(8,128)S(1)}, f32[5,32,128]{2,1,0:T(8,128)S(1)}, u32[]{:S(2)}, u32[]{:S(2)}) collective-permute-start(f32[5,32,128]{2,1,0:T(8,128)S(1)} %get-tuple-element.36), channel_id=1, source_target_pairs={{3,32},{4,33},{5,34},{6,35},{7,36},{8,37},{9,38},{10,39},{11,40},{... | collective-permute-start | bytes 245768 | tf_op jit(solution)/shard_map/ppermute | solution.py:75
  253.1 19.7 %collective-permute-start.64 = (f32[5,32,128]{2,1,0:T(8,128)S(1)}, f32[5,32,128]{2,1,0:T(8,128)S(1)}, u32[]{:S(2)}, u32[]{:S(2)}) collective-permute-start(f32[5,32,128]{2,1,0:T(8,128)S(1)} %get-tuple-element.36), channel_id=1, source_target_pairs={{4,32},{5,33},{6,34},{7,35},{8,36},{9,37},{10,38},{11,39},{12,40},... | collective-permute-start | bytes 245768 | tf_op jit(solution)/shard_map/ppermute | solution.py:75
  269.0 17.7 %collective-permute-start.67 = (f32[5,32,128]{2,1,0:T(8,128)S(1)}, f32[5,32,128]{2,1,0:T(8,128)S(1)}, u32[]{:S(2)}, u32[]{:S(2)}) collective-permute-start(f32[5,32,128]{2,1,0:T(8,128)S(1)} %get-tuple-element.36), channel_id=1, source_target_pairs={{7,32},{8,33},{9,34},{10,35},{11,36},{12,37},{13,38},{14,39},{15,4... | collective-permute-start | bytes 245768 | tf_op jit(solution)/shard_map/ppermute | solution.py:75
  272.8 17.7 %collective-permute-start.69 = (f32[5,32,128]{2,1,0:T(8,128)S(1)}, f32[5,32,128]{2,1,0:T(8,128)S(1)}, u32[]{:S(2)}, u32[]{:S(2)}) collective-permute-start(f32[5,32,128]{2,1,0:T(8,128)S(1)} %get-tuple-element.36), channel_id=1, source_target_pairs={{9,32},{10,33},{11,34},{12,35},{13,36},{14,37},{15,38},{16,39},{17... | collective-permute-start | bytes 245768 | tf_op jit(solution)/shard_map/ppermute | solution.py:75
  310.5 30.1 %collective-permute-start.70 = (f32[2,3,5,32,128]{4,3,2,1,0:T(8,128)}, f32[2,3,5,32,128]{4,3,2,1,0:T(8,128)}, u32[]{:S(2)}, u32[]{:S(2)}) collective-permute-start(f32[2,3,5,32,128]{4,3,2,1,0:T(8,128)} %pad_maximum_fusion.20), channel_id=1, source_target_pairs={{8,0},{9,1},{10,2},{11,3},{12,4},{13,5},{14,6},{15,7},{16,8},{17,9... | collective-permute-start | bytes 1474568 | tf_op jit(solution)/shard_map/ppermute | solution.py:78
  311.9 28.8 %collective-permute-start.71 = (f32[2,3,5,32,128]{4,3,2,1,0:T(8,128)}, f32[2,3,5,32,128]{4,3,2,1,0:T(8,128)}, u32[]{:S(2)}, u32[]{:S(2)}) collective-permute-start(f32[2,3,5,32,128]{4,3,2,1,0:T(8,128)} %pad_maximum_fusion.20), channel_id=1, source_target_pairs={{16,0},{17,1},{18,2},{19,3},{20,4},{21,5},{22,6},{23,7},{24,8},{25... | collective-permute-start | bytes 1474568 | tf_op jit(solution)/shard_map/ppermute | solution.py:78
  312.0 28.7 %collective-permute-start.72 = (f32[2,3,5,32,128]{4,3,2,1,0:T(8,128)}, f32[2,3,5,32,128]{4,3,2,1,0:T(8,128)}, u32[]{:S(2)}, u32[]{:S(2)}) collective-permute-start(f32[2,3,5,32,128]{4,3,2,1,0:T(8,128)} %pad_maximum_fusion.20), channel_id=1, source_target_pairs={{24,0},{25,1},{26,2},{27,3},{28,4},{29,5},{30,6},{31,7},{0,8},{1,9... | collective-permute-start | bytes 1474568 | tf_op jit(solution)/shard_map/ppermute | solution.py:78
  (87 other events, 978.0 us)
where the time goes:
time: 353 us; the launch traced here: 349 us
  starting transfers between devices  173 us (49%)
  local copies, waits for them, and re-layouts  49.1 us (14%)
  waiting for transfers between devices  48.5 us (14%)
  between operations  42.1 us (12%)
  other arithmetic  32.4 us (9%)
  matrix products  4.03 us (1%)
    ppermute x60, starting transfers between devices, from_row(): return lax.ppermute(plane, ('row', 'circ'), pairs)  150 us
    ppermute x60, waiting for transfers between devices, from_row(): return lax.ppermute(plane, ('row', 'circ'), pairs)  18.6 us
    ppermute x3, starting transfers between devices, extended(): lax.ppermute(head, axis, [((i + 1) % count, i) for i in range(count)])  12.8 us
    slice x5, local copies, waits for them, and re-layouts, extended(): lax.slice_in_dim(cells, cells.shape[dim] - width, cells.shape[dim], axis=...  12.4 us
    ppermute x3, waiting for transfers between devices, extended(): lax.ppermute(head, axis, [((i + 1) % count, i) for i in range(count)])  10.3 us
    ppermute x3, waiting for transfers between devices, extended(): lax.ppermute(tail, axis, [(i, (i + 1) % count) for i in range(count)])  9.94 us
    ppermute x9, starting transfers between devices, along_circ(): lax.ppermute(value, 'circ', [((b + shift) % loop_size, b) for b in range(...  9.93 us
    ppermute x9, waiting for transfers between devices, along_circ(): lax.ppermute(value, 'circ', [((b + shift) % loop_size, b) for b in range(...  9.59 us
  transfers between devices with their start and end apart: 75, of which 20 were waited for; matrix products, arithmetic and copies ran while one was open for 16% of the time, Pallas kernels for 0%

commit v1 on v0

--- a/solution.py
+++ b/solution.py
@@ -25,32 +25,25 @@
     return cells
 
 
-def combine(fields, axial_ext, radial_ext, around_ext, velocity):
-    d_axial = 0.5 * (axial_ext[:, 2:] - axial_ext[:, :-2])
-    d_radial = 0.5 * (radial_ext[:, :, 2:] - radial_ext[:, :, :-2])
-    d_around = 0.5 * (around_ext[..., 2:] - around_ext[..., :-2])
+def tendency(center, below, above, around, velocity):
+    radial = jnp.concatenate([center[:, :, :1], center, center[:, :, -1:]], axis=2)
+    d_axial = 0.5 * (above - below)
+    d_radial = 0.5 * (radial[:, :, 2:] - radial[:, :, :-2])
+    d_around = 0.5 * (around[..., 2:] - around[..., :-2])
     laplace = (
-        axial_ext[:, 2:]
-        + axial_ext[:, :-2]
-        + radial_ext[:, :, 2:]
-        + radial_ext[:, :, :-2]
-        + around_ext[..., 2:]
-        + around_ext[..., :-2]
-        - 6.0 * fields
+        above
+        + below
+        + radial[:, :, 2:]
+        + radial[:, :, :-2]
+        + around[..., 2:]
+        + around[..., :-2]
+        - 6.0 * center
     )
     strain = jnp.sum(d_axial[1:4] ** 2 + d_radial[1:4] ** 2 + d_around[1:4] ** 2, axis=0)
     eddy_visc = SMAG_COEF * jnp.sqrt(strain + 1.0)
     return eddy_visc * laplace - (
         velocity[0] * d_axial + velocity[1] * d_radial + velocity[2] * d_around
     )
-
-
-def radial_pad(fields):
-    return jnp.concatenate([fields[:, :, :1], fields, fields[:, :, -1:]], axis=2)
-
-
-def axial_pad(fields, lower_ghost, upper_ghost):
-    return jnp.concatenate([lower_ghost[:, None], fields, upper_ghost[:, None]], axis=1)
 
 
 def local(flow_state, velocity, offsets, passage_shift, donor_step, donor_weight):
@@ -124,24 +117,42 @@
         ]
         return out[0], out[1]
 
-    def evaluate_section(fields, section_index):
-        first_plane = fields[:, 0]
-        last_plane = fields[:, -1]
-        around_ext = extended(fields, (("circ", 3),), 1)
-        lower_ghost, upper_ghost = ghosts(last_plane, first_plane, section_index)
-        lower_ghost = jnp.where(row_id == 0, first_plane, lower_ghost)
-        upper_ghost = jnp.where(row_id == row_count - 1, last_plane, upper_ghost)
-        return combine(
-            fields,
-            axial_pad(fields, lower_ghost, upper_ghost),
-            radial_pad(fields),
-            around_ext,
-            velocity,
+    def section(fields, first_plane, last_plane, section_index, base_scale, step_scale):
+        around = extended(fields, (("circ", 3),), 1)
+        lower, upper = ghosts(last_plane, first_plane, section_index)
+        lower = jnp.where(row_id == 0, first_plane, lower)
+        upper = jnp.where(row_id == row_count - 1, last_plane, upper)
+
+        def advance(start, now, rate):
+            if base_scale is None:
+                return now + TIME_STEP * rate
+            return base_scale * start + step_scale * (now + TIME_STEP * rate)
+
+        head = advance(
+            flow_state[:, :1],
+            fields[:, :1],
+            tendency(fields[:, :1], lower[:, None], fields[:, 1:2], around[:, :1], velocity[:, :1]),
         )
+        tail = advance(
+            flow_state[:, -1:],
+            fields[:, -1:],
+            tendency(
+                fields[:, -1:], fields[:, -2:-1], upper[:, None], around[:, -1:], velocity[:, -1:]
+            ),
+        )
+        inner = advance(
+            flow_state[:, 1:-1],
+            fields[:, 1:-1],
+            tendency(
+                fields[:, 1:-1], fields[:, :-2], fields[:, 2:], around[:, 1:-1], velocity[:, 1:-1]
+            ),
+        )
+        return jnp.concatenate([head, inner, tail], axis=1), head[:, 0], tail[:, 0]
 
-    section_one = flow_state + TIME_STEP * evaluate_section(flow_state, 0)
-    section_two = 0.75 * flow_state + 0.25 * (section_one + TIME_STEP * evaluate_section(section_one, 1))
-    return 1.0 / 3.0 * flow_state + 2.0 / 3.0 * (section_two + TIME_STEP * evaluate_section(section_two, 2))
+    v1, f1, l1 = section(flow_state, flow_state[:, 0], flow_state[:, -1], 0, None, None)
+    v2, f2, l2 = section(v1, f1, l1, 1, 0.75, 0.25)
+    v3, _, _ = section(v2, f2, l2, 2, 1.0 / 3.0, 2.0 / 3.0)
+    return v3
 
 
 def solution(mesh):

time: 353 us -> 373 us (1.057)
  the two profiles are of different devices: /device:TPU:1 before, /device:TPU:40 now
where the time goes in v1:
time: 373 us; the launch traced here: 365 us
  starting transfers between devices  138 us (37%)
  waiting for transfers between devices  105 us (28%)
  local copies, waits for them, and re-layouts  45.8 us (12%)
  between operations  41.4 us (11%)
  other arithmetic  31.3 us (8%)
  matrix products  3.99 us (1%)
    ppermute x60, starting transfers between devices, from_row(): return lax.ppermute(plane, ('row', 'circ'), pairs)  120 us
    ppermute x9, waiting for transfers between devices, along_circ(): lax.ppermute(value, 'circ', [((b + shift) % loop_size, b) for b in range(...  66.3 us
    ppermute x60, waiting for transfers between devices, from_row(): return lax.ppermute(plane, ('row', 'circ'), pairs)  37.6 us
    slice x5, local copies, waits for them, and re-layouts, extended(): head = lax.slice_in_dim(cells, 0, width, axis=dim)  11.7 us
    ppermute x3, starting transfers between devices, extended(): lax.ppermute(head, axis, [((i + 1) % count, i) for i in range(count)])  9.64 us
  transfers between devices with their start and end apart: 75, of which 29 were waited for; matrix products, arithmetic and copies ran while one was open for 19% of the time, Pallas kernels for 0%

profile of v1, /device:TPU:40, one launch (start us, length us, event | category | flops | bytes accessed | tf_op | source)
XLA Modules:
  0.0 365.4 jit_solution(6513598488495902793)
XLA Ops:
  3.4 5.8 %collective-permute-start.1 = (f32[5,32,128]{2,1,0:T(8,128)}, f32[5,32,128]{2,1,0:T(8,128)S(1)}, u32[]{:S(2)}, u32[]{:S(2)}) collective-permute-start(f32[5,32,128]{2,1,0:T(8,128)} %get-tuple-element.78), channel_id=1, source_target_pairs={{1,32},{2,33},{3,34},{4,35},{5,36},{6,37},{7,38},{8,39},{9,40},{10... | collective-permute-start | bytes 245768 | tf_op jit(solution)/shard_map/ppermute | solution.py:68
  11.2 3.3 fusion.97
  14.4 2.6 copy.82
  17.0 5.8 %collective-permute-start.23 = (f32[5,16,32,1]{2,1,3,0:T(8,128)}, f32[5,16,32,1]{2,1,3,0:T(8,128)}, u32[]{:S(2)}, u32[]{:S(2)}) collective-permute-start(f32[5,16,32,1]{2,1,3,0:T(8,128)} %copy.82), channel_id=1, source_target_pairs={{1,0},{2,1},{3,2},{4,3},{5,4},{6,5},{7,6},{8,7},{9,8},{10,9},{11,1... | collective-permute-start | bytes 30728 | tf_op jit(solution)/shard_map/ppermute | solution.py:21
  33.2 2.6 and_select_fusion.2
  78.8 3.2 collective-permute-start.3
  83.4 4.7 %collective-permute-start.4 = (f32[5,32,128]{2,1,0:T(8,128)}, f32[5,32,128]{2,1,0:T(8,128)}, u32[]{:S(2)}, u32[]{:S(2)}) collective-permute-start(f32[5,32,128]{2,1,0:T(8,128)} %get-tuple-element.78), channel_id=1, source_target_pairs={{4,32},{5,33},{6,34},{7,35},{8,36},{9,37},{10,38},{11,39},{12,40},... | collective-permute-start | bytes 245768 | tf_op jit(solution)/shard_map/ppermute | solution.py:68
  117.4 3.6 collective-permute-done.15
  125.9 3.4 collective-permute-done.19
  133.3 8.2 %collective-permute-done.20 = f32[2,3,5,32,128]{4,3,2,1,0:T(8,128)S(1)} collective-permute-done((f32[2,3,5,32,128]{4,3,2,1,0:T(8,128)S(1)}, f32[2,3,5,32,128]{4,3,2,1,0:T(8,128)S(1)}, u32[]{:S(2)}, u32[]{:S(2)}) %collective-permute-start.20) | collective-permute-done | bytes 491552 | tf_op jit(solution)/shard_map/ppermute | solution.py:71
  141.5 3.0 collective-permute-done.21
  144.5 11.9 %collective-permute-done.22 = f32[2,3,5,32,128]{4,3,2,1,0:T(8,128)S(1)} collective-permute-done((f32[2,3,5,32,128]{4,3,2,1,0:T(8,128)S(1)}, f32[2,3,5,32,128]{4,3,2,1,0:T(8,128)S(1)}, u32[]{:S(2)}, u32[]{:S(2)}) %collective-permute-start.22) | collective-permute-done | bytes 491552 | tf_op jit(solution)/shard_map/ppermute | solution.py:71
  161.9 7.1 %collective-permute-start.26 = (f32[5,32,128]{2,1,0:T(8,128)S(1)}, f32[5,32,128]{2,1,0:T(8,128)S(1)}, u32[]{:S(2)}, u32[]{:S(2)}) collective-permute-start(f32[5,32,128]{2,1,0:T(8,128)S(1)} %bitcast.308), channel_id=1, source_target_pairs={{1,32},{2,33},{3,34},{4,35},{5,36},{6,37},{7,38},{8,39},{9,40},{10... | collective-permute-start | bytes 245768 | tf_op jit(solution)/shard_map/ppermute | solution.py:68
  169.0 2.7 collective-permute-start.27
  186.8 4.4 %collective-permute-start.29 = (f32[5,32,128]{2,1,0:T(8,128)S(1)}, f32[5,32,128]{2,1,0:T(8,128)}, u32[]{:S(2)}, u32[]{:S(2)}) collective-permute-start(f32[5,32,128]{2,1,0:T(8,128)S(1)} %bitcast.311), channel_id=1, source_target_pairs={{4,32},{5,33},{6,34},{7,35},{8,36},{9,37},{10,38},{11,39},{12,40},... | collective-permute-start | bytes 245768 | tf_op jit(solution)/shard_map/ppermute | solution.py:68
  193.5 2.8 fusion.3
  199.3 3.1 collective-permute-start.32
  220.9 3.6 collective-permute-done.40
  228.7 3.5 collective-permute-done.44
  235.1 2.7 multiply_add_fusion.1
  238.0 5.9 %collective-permute-done.45 = f32[2,3,5,32,128]{4,3,2,1,0:T(8,128)S(1)} collective-permute-done((f32[2,3,5,32,128]{4,3,2,1,0:T(8,128)S(1)}, f32[2,3,5,32,128]{4,3,2,1,0:T(8,128)S(1)}, u32[]{:S(2)}, u32[]{:S(2)}) %collective-permute-start.45) | collective-permute-done | bytes 491552 | tf_op jit(solution)/shard_map/ppermute | solution.py:71
  245.8 13.5 %collective-permute-done.47 = f32[2,3,5,32,128]{4,3,2,1,0:T(8,128)S(1)} collective-permute-done((f32[2,3,5,32,128]{4,3,2,1,0:T(8,128)S(1)}, f32[2,3,5,32,128]{4,3,2,1,0:T(8,128)S(1)}, u32[]{:S(2)}, u32[]{:S(2)}) %collective-permute-start.47) | collective-permute-done | bytes 491552 | tf_op jit(solution)/shard_map/ppermute | solution.py:71
  261.9 2.7 collective-permute-start.50
  264.6 7.6 %collective-permute-start.51 = (f32[5,32,128]{2,1,0:T(8,128)S(1)}, f32[5,32,128]{2,1,0:T(8,128)}, u32[]{:S(2)}, u32[]{:S(2)}) collective-permute-start(f32[5,32,128]{2,1,0:T(8,128)S(1)} %bitcast.278), channel_id=1, source_target_pairs={{1,32},{2,33},{3,34},{4,35},{5,36},{6,37},{7,38},{8,39},{9,40},{10... | collective-permute-start | bytes 245768 | tf_op jit(solution)/shard_map/ppermute | solution.py:68
  287.3 4.3 %collective-permute-start.54 = (f32[5,32,128]{2,1,0:T(8,128)S(1)}, f32[5,32,128]{2,1,0:T(8,128)S(1)}, u32[]{:S(2)}, u32[]{:S(2)}) collective-permute-start(f32[5,32,128]{2,1,0:T(8,128)S(1)} %bitcast.281), channel_id=1, source_target_pairs={{4,32},{5,33},{6,34},{7,35},{8,36},{9,37},{10,38},{11,39},{12,40},... | collective-permute-start | bytes 245768 | tf_op jit(solution)/shard_map/ppermute | solution.py:68
  294.0 2.8 fusion.4
  300.7 2.9 collective-permute-start.57
  322.3 3.7 %collective-permute-done.65 = f32[5,32,128]{2,1,0:T(8,128)S(1)} collective-permute-done((f32[5,32,128]{2,1,0:T(8,128)S(1)}, f32[5,32,128]{2,1,0:T(8,128)S(1)}, u32[]{:S(2)}, u32[]{:S(2)}) %collective-permute-start.65) | collective-permute-done | bytes 81952 | tf_op jit(solution)/shard_map/ppermute | solution.py:68
  330.8 3.5 collective-permute-done.69
  336.6 2.7 multiply_add_fusion
  339.2 7.4 %collective-permute-done.70 = f32[2,3,5,32,128]{4,3,2,1,0:T(8,128)S(1)} collective-permute-done((f32[2,3,5,32,128]{4,3,2,1,0:T(8,128)S(1)}, f32[2,3,5,32,128]{4,3,2,1,0:T(8,128)S(1)}, u32[]{:S(2)}, u32[]{:S(2)}) %collective-permute-start.70) | collective-permute-done | bytes 491552 | tf_op jit(solution)/shard_map/ppermute | solution.py:71
  348.5 12.7 %collective-permute-done.72 = f32[2,3,5,32,128]{4,3,2,1,0:T(8,128)S(1)} collective-permute-done((f32[2,3,5,32,128]{4,3,2,1,0:T(8,128)S(1)}, f32[2,3,5,32,128]{4,3,2,1,0:T(8,128)S(1)}, u32[]{:S(2)}, u32[]{:S(2)}) %collective-permute-start.72) | collective-permute-done | bytes 491552 | tf_op jit(solution)/shard_map/ppermute | solution.py:71
  (339 shorter events, 166.5 us)
Async XLA Ops:
  1.6 91.8 %collective-permute-start = (f32[5,32,128]{2,1,0:T(8,128)}, f32[5,32,128]{2,1,0:T(8,128)S(1)}, u32[]{:S(2)}, u32[]{:S(2)}) collective-permute-start(f32[5,32,128]{2,1,0:T(8,128)} %get-tuple-element.78), channel_id=1, source_target_pairs={{0,32},{1,33},{2,34},{3,35},{4,36},{5,37},{6,38},{7,39},{8,40},{9,... | collective-permute-start | bytes 245768 | tf_op jit(solution)/shard_map/ppermute | solution.py:68
  3.4 92.3 %collective-permute-start.1 = (f32[5,32,128]{2,1,0:T(8,128)}, f32[5,32,128]{2,1,0:T(8,128)S(1)}, u32[]{:S(2)}, u32[]{:S(2)}) collective-permute-start(f32[5,32,128]{2,1,0:T(8,128)} %get-tuple-element.78), channel_id=1, source_target_pairs={{1,32},{2,33},{3,34},{4,35},{5,36},{6,37},{7,38},{8,39},{9,40},{10... | collective-permute-start | bytes 245768 | tf_op jit(solution)/shard_map/ppermute | solution.py:68
  9.1 87.8 %collective-permute-start.2 = (f32[5,32,128]{2,1,0:T(8,128)}, f32[5,32,128]{2,1,0:T(8,128)}, u32[]{:S(2)}, u32[]{:S(2)}) collective-permute-start(f32[5,32,128]{2,1,0:T(8,128)} %get-tuple-element.78), channel_id=1, source_target_pairs={{2,32},{3,33},{4,34},{5,35},{6,36},{7,37},{8,38},{9,39},{10,40},{1... | collective-permute-start | bytes 245768 | tf_op jit(solution)/shard_map/ppermute | solution.py:68
  17.0 61.8 %collective-permute-start.23 = (f32[5,16,32,1]{2,1,3,0:T(8,128)}, f32[5,16,32,1]{2,1,3,0:T(8,128)}, u32[]{:S(2)}, u32[]{:S(2)}) collective-permute-start(f32[5,16,32,1]{2,1,3,0:T(8,128)} %copy.82), channel_id=1, source_target_pairs={{1,0},{2,1},{3,2},{4,3},{5,4},{6,5},{7,6},{8,7},{9,8},{10,9},{11,1... | collective-permute-start | bytes 30728 | tf_op jit(solution)/shard_map/ppermute | solution.py:21
  24.0 59.4 %collective-permute-start.24 = (f32[5,16,32,1]{2,1,3,0:T(8,128)}, f32[5,16,32,1]{2,1,3,0:T(8,128)}, u32[]{:S(2)}, u32[]{:S(2)}) collective-permute-start(f32[5,16,32,1]{2,1,3,0:T(8,128)} %copy.83), channel_id=1, source_target_pairs={{0,1},{1,2},{2,3},{3,4},{4,5},{5,6},{6,7},{7,8},{8,9},{9,10},{10,1... | collective-permute-start | bytes 30728 | tf_op jit(solution)/shard_map/ppermute | solution.py:19
  78.8 19.9 %collective-permute-start.3 = (f32[5,32,128]{2,1,0:T(8,128)}, f32[5,32,128]{2,1,0:T(8,128)}, u32[]{:S(2)}, u32[]{:S(2)}) collective-permute-start(f32[5,32,128]{2,1,0:T(8,128)} %get-tuple-element.78), channel_id=1, source_target_pairs={{3,32},{4,33},{5,34},{6,35},{7,36},{8,37},{9,38},{10,39},{11,40},{... | collective-permute-start | bytes 245768 | tf_op jit(solution)/shard_map/ppermute | solution.py:68
  83.4 16.7 %collective-permute-start.4 = (f32[5,32,128]{2,1,0:T(8,128)}, f32[5,32,128]{2,1,0:T(8,128)}, u32[]{:S(2)}, u32[]{:S(2)}) collective-permute-start(f32[5,32,128]{2,1,0:T(8,128)} %get-tuple-element.78), channel_id=1, source_target_pairs={{4,32},{5,33},{6,34},{7,35},{8,36},{9,37},{10,38},{11,39},{12,40},... | collective-permute-start | bytes 245768 | tf_op jit(solution)/shard_map/ppermute | solution.py:68
  116.1 13.3 %collective-permute-start.19 = (f32[5,32,128]{2,1,0:T(8,128)S(1)}, f32[5,32,128]{2,1,0:T(8,128)S(1)}, u32[]{:S(2)}, u32[]{:S(2)}) collective-permute-start(f32[5,32,128]{2,1,0:T(8,128)S(1)} %copy-done.38), channel_id=1, source_target_pairs={{41,0},{42,1},{43,2},{44,3},{45,4},{46,5},{47,6},{48,7},{49,8},{50... | collective-permute-start | bytes 245768 | tf_op jit(solution)/shard_map/ppermute | solution.py:68
  129.5 12.0 %collective-permute-start.20 = (f32[2,3,5,32,128]{4,3,2,1,0:T(8,128)S(1)}, f32[2,3,5,32,128]{4,3,2,1,0:T(8,128)S(1)}, u32[]{:S(2)}, u32[]{:S(2)}) collective-permute-start(f32[2,3,5,32,128]{4,3,2,1,0:T(8,128)S(1)} %pad_maximum_fusion.19), channel_id=1, source_target_pairs={{8,0},{9,1},{10,2},{11,3},{12,4},{13,5},{14,6},{15,7},{16,8},{17,9... | collective-permute-start | bytes 1474568 | tf_op jit(solution)/shard_map/ppermute | solution.py:71
  130.4 14.1 %collective-permute-start.21 = (f32[2,3,5,32,128]{4,3,2,1,0:T(8,128)S(1)}, f32[2,3,5,32,128]{4,3,2,1,0:T(8,128)S(1)}, u32[]{:S(2)}, u32[]{:S(2)}) collective-permute-start(f32[2,3,5,32,128]{4,3,2,1,0:T(8,128)S(1)} %pad_maximum_fusion.19), channel_id=1, source_target_pairs={{16,0},{17,1},{18,2},{19,3},{20,4},{21,5},{22,6},{23,7},{24,8},{25... | collective-permute-start | bytes 1474568 | tf_op jit(solution)/shard_map/ppermute | solution.py:71
  131.4 25.1 %collective-permute-start.22 = (f32[2,3,5,32,128]{4,3,2,1,0:T(8,128)S(1)}, f32[2,3,5,32,128]{4,3,2,1,0:T(8,128)S(1)}, u32[]{:S(2)}, u32[]{:S(2)}) collective-permute-start(f32[2,3,5,32,128]{4,3,2,1,0:T(8,128)S(1)} %pad_maximum_fusion.19), channel_id=1, source_target_pairs={{24,0},{25,1},{26,2},{27,3},{28,4},{29,5},{30,6},{31,7},{0,8},{1,9... | collective-permute-start | bytes 1474568 | tf_op jit(solution)/shard_map/ppermute | solution.py:71
  159.9 36.8 %collective-permute-start.25 = (f32[5,32,128]{2,1,0:T(8,128)S(1)}, f32[5,32,128]{2,1,0:T(8,128)S(1)}, u32[]{:S(2)}, u32[]{:S(2)}) collective-permute-start(f32[5,32,128]{2,1,0:T(8,128)S(1)} %bitcast.307), channel_id=1, source_target_pairs={{0,32},{1,33},{2,34},{3,35},{4,36},{5,37},{6,38},{7,39},{8,40},{9,... | collective-permute-start | bytes 245768 | tf_op jit(solution)/shard_map/ppermute | solution.py:68
  161.9 36.1 %collective-permute-start.26 = (f32[5,32,128]{2,1,0:T(8,128)S(1)}, f32[5,32,128]{2,1,0:T(8,128)S(1)}, u32[]{:S(2)}, u32[]{:S(2)}) collective-permute-start(f32[5,32,128]{2,1,0:T(8,128)S(1)} %bitcast.308), channel_id=1, source_target_pairs={{1,32},{2,33},{3,34},{4,35},{5,36},{6,37},{7,38},{8,39},{9,40},{10... | collective-permute-start | bytes 245768 | tf_op jit(solution)/shard_map/ppermute | solution.py:68
  169.0 30.3 %collective-permute-start.27 = (f32[5,32,128]{2,1,0:T(8,128)S(1)}, f32[5,32,128]{2,1,0:T(8,128)}, u32[]{:S(2)}, u32[]{:S(2)}) collective-permute-start(f32[5,32,128]{2,1,0:T(8,128)S(1)} %bitcast.309), channel_id=1, source_target_pairs={{2,32},{3,33},{4,34},{5,35},{6,36},{7,37},{8,38},{9,39},{10,40},{1... | collective-permute-start | bytes 245768 | tf_op jit(solution)/shard_map/ppermute | solution.py:68
  182.2 20.2 %collective-permute-start.28 = (f32[5,32,128]{2,1,0:T(8,128)S(1)}, f32[5,32,128]{2,1,0:T(8,128)}, u32[]{:S(2)}, u32[]{:S(2)}) collective-permute-start(f32[5,32,128]{2,1,0:T(8,128)S(1)} %bitcast.310), channel_id=1, source_target_pairs={{3,32},{4,33},{5,34},{6,35},{7,36},{8,37},{9,38},{10,39},{11,40},{... | collective-permute-start | bytes 245768 | tf_op jit(solution)/shard_map/ppermute | solution.py:68
  186.8 17.0 %collective-permute-start.29 = (f32[5,32,128]{2,1,0:T(8,128)S(1)}, f32[5,32,128]{2,1,0:T(8,128)}, u32[]{:S(2)}, u32[]{:S(2)}) collective-permute-start(f32[5,32,128]{2,1,0:T(8,128)S(1)} %bitcast.311), channel_id=1, source_target_pairs={{4,32},{5,33},{6,34},{7,35},{8,36},{9,37},{10,38},{11,39},{12,40},... | collective-permute-start | bytes 245768 | tf_op jit(solution)/shard_map/ppermute | solution.py:68
  213.2 11.3 %collective-permute-start.40 = (f32[5,32,128]{2,1,0:T(8,128)S(1)}, f32[5,32,128]{2,1,0:T(8,128)S(1)}, u32[]{:S(2)}, u32[]{:S(2)}) collective-permute-start(f32[5,32,128]{2,1,0:T(8,128)S(1)} %bitcast.302), channel_id=1, source_target_pairs={{37,0},{38,1},{39,2},{40,3},{41,4},{42,5},{43,6},{44,7},{45,8},{46... | collective-permute-start | bytes 245768 | tf_op jit(solution)/shard_map/ppermute | solution.py:68
  215.8 11.4 %collective-permute-start.42 = (f32[5,32,128]{2,1,0:T(8,128)S(1)}, f32[5,32,128]{2,1,0:T(8,128)S(1)}, u32[]{:S(2)}, u32[]{:S(2)}) collective-permute-start(f32[5,32,128]{2,1,0:T(8,128)S(1)} %bitcast.304), channel_id=1, source_target_pairs={{39,0},{40,1},{41,2},{42,3},{43,4},{44,5},{45,6},{46,7},{47,8},{48... | collective-permute-start | bytes 245768 | tf_op jit(solution)/shard_map/ppermute | solution.py:68
  219.6 12.7 %collective-permute-start.44 = (f32[5,32,128]{2,1,0:T(8,128)S(1)}, f32[5,32,128]{2,1,0:T(8,128)S(1)}, u32[]{:S(2)}, u32[]{:S(2)}) collective-permute-start(f32[5,32,128]{2,1,0:T(8,128)S(1)} %bitcast.306), channel_id=1, source_target_pairs={{41,0},{42,1},{43,2},{44,3},{45,4},{46,5},{47,6},{48,7},{49,8},{50... | collective-permute-start | bytes 245768 | tf_op jit(solution)/shard_map/ppermute | solution.py:68
  232.4 11.5 %collective-permute-start.45 = (f32[2,3,5,32,128]{4,3,2,1,0:T(8,128)S(1)}, f32[2,3,5,32,128]{4,3,2,1,0:T(8,128)S(1)}, u32[]{:S(2)}, u32[]{:S(2)}) collective-permute-start(f32[2,3,5,32,128]{4,3,2,1,0:T(8,128)S(1)} %pad_maximum_fusion.20), channel_id=1, source_target_pairs={{8,0},{9,1},{10,2},{11,3},{12,4},{13,5},{14,6},{15,7},{16,8},{17,9... | collective-permute-start | bytes 1474568 | tf_op jit(solution)/shard_map/ppermute | solution.py:71
  233.2 12.6 %collective-permute-start.46 = (f32[2,3,5,32,128]{4,3,2,1,0:T(8,128)S(1)}, f32[2,3,5,32,128]{4,3,2,1,0:T(8,128)S(1)}, u32[]{:S(2)}, u32[]{:S(2)}) collective-permute-start(f32[2,3,5,32,128]{4,3,2,1,0:T(8,128)S(1)} %pad_maximum_fusion.20), channel_id=1, source_target_pairs={{16,0},{17,1},{18,2},{19,3},{20,4},{21,5},{22,6},{23,7},{24,8},{25... | collective-permute-start | bytes 1474568 | tf_op jit(solution)/shard_map/ppermute | solution.py:71
  234.5 24.8 %collective-permute-start.47 = (f32[2,3,5,32,128]{4,3,2,1,0:T(8,128)S(1)}, f32[2,3,5,32,128]{4,3,2,1,0:T(8,128)S(1)}, u32[]{:S(2)}, u32[]{:S(2)}) collective-permute-start(f32[2,3,5,32,128]{4,3,2,1,0:T(8,128)S(1)} %pad_maximum_fusion.20), channel_id=1, source_target_pairs={{24,0},{25,1},{26,2},{27,3},{28,4},{29,5},{30,6},{31,7},{0,8},{1,9... | collective-permute-start | bytes 1474568 | tf_op jit(solution)/shard_map/ppermute | solution.py:71
  261.9 35.3 %collective-permute-start.50 = (f32[5,32,128]{2,1,0:T(8,128)S(1)}, f32[5,32,128]{2,1,0:T(8,128)}, u32[]{:S(2)}, u32[]{:S(2)}) collective-permute-start(f32[5,32,128]{2,1,0:T(8,128)S(1)} %bitcast.277), channel_id=1, source_target_pairs={{0,32},{1,33},{2,34},{3,35},{4,36},{5,37},{6,38},{7,39},{8,40},{9,... | collective-permute-start | bytes 245768 | tf_op jit(solution)/shard_map/ppermute | solution.py:68
  264.6 34.8 %collective-permute-start.51 = (f32[5,32,128]{2,1,0:T(8,128)S(1)}, f32[5,32,128]{2,1,0:T(8,128)}, u32[]{:S(2)}, u32[]{:S(2)}) collective-permute-start(f32[5,32,128]{2,1,0:T(8,128)S(1)} %bitcast.278), channel_id=1, source_target_pairs={{1,32},{2,33},{3,34},{4,35},{5,36},{6,37},{7,38},{8,39},{9,40},{10... | collective-permute-start | bytes 245768 | tf_op jit(solution)/shard_map/ppermute | solution.py:68
  272.1 28.5 %collective-permute-start.52 = (f32[5,32,128]{2,1,0:T(8,128)S(1)}, f32[5,32,128]{2,1,0:T(8,128)}, u32[]{:S(2)}, u32[]{:S(2)}) collective-permute-start(f32[5,32,128]{2,1,0:T(8,128)S(1)} %bitcast.279), channel_id=1, source_target_pairs={{2,32},{3,33},{4,34},{5,35},{6,36},{7,37},{8,38},{9,39},{10,40},{1... | collective-permute-start | bytes 245768 | tf_op jit(solution)/shard_map/ppermute | solution.py:68
  283.7 20.0 %collective-permute-start.53 = (f32[5,32,128]{2,1,0:T(8,128)S(1)}, f32[5,32,128]{2,1,0:T(8,128)S(1)}, u32[]{:S(2)}, u32[]{:S(2)}) collective-permute-start(f32[5,32,128]{2,1,0:T(8,128)S(1)} %bitcast.280), channel_id=1, source_target_pairs={{3,32},{4,33},{5,34},{6,35},{7,36},{8,37},{9,38},{10,39},{11,40},{... | collective-permute-start | bytes 245768 | tf_op jit(solution)/shard_map/ppermute | solution.py:68
  287.3 17.6 %collective-permute-start.54 = (f32[5,32,128]{2,1,0:T(8,128)S(1)}, f32[5,32,128]{2,1,0:T(8,128)S(1)}, u32[]{:S(2)}, u32[]{:S(2)}) collective-permute-start(f32[5,32,128]{2,1,0:T(8,128)S(1)} %bitcast.281), channel_id=1, source_target_pairs={{4,32},{5,33},{6,34},{7,35},{8,36},{9,37},{10,38},{11,39},{12,40},... | collective-permute-start | bytes 245768 | tf_op jit(solution)/shard_map/ppermute | solution.py:68
  319.6 11.2 %collective-permute-start.68 = (f32[5,32,128]{2,1,0:T(8,128)S(1)}, f32[5,32,128]{2,1,0:T(8,128)S(1)}, u32[]{:S(2)}, u32[]{:S(2)}) collective-permute-start(f32[5,32,128]{2,1,0:T(8,128)S(1)} %bitcast.295), channel_id=1, source_target_pairs={{40,0},{41,1},{42,2},{43,3},{44,4},{45,5},{46,6},{47,7},{48,8},{49... | collective-permute-start | bytes 245768 | tf_op jit(solution)/shard_map/ppermute | solution.py:68
  320.9 13.4 %collective-permute-start.69 = (f32[5,32,128]{2,1,0:T(8,128)S(1)}, f32[5,32,128]{2,1,0:T(8,128)S(1)}, u32[]{:S(2)}, u32[]{:S(2)}) collective-permute-start(f32[5,32,128]{2,1,0:T(8,128)S(1)} %bitcast.296), channel_id=1, source_target_pairs={{41,0},{42,1},{43,2},{44,3},{45,4},{46,5},{47,6},{48,7},{49,8},{50... | collective-permute-start | bytes 245768 | tf_op jit(solution)/shard_map/ppermute | solution.py:68
  334.5 12.2 %collective-permute-start.70 = (f32[2,3,5,32,128]{4,3,2,1,0:T(8,128)S(1)}, f32[2,3,5,32,128]{4,3,2,1,0:T(8,128)S(1)}, u32[]{:S(2)}, u32[]{:S(2)}) collective-permute-start(f32[2,3,5,32,128]{4,3,2,1,0:T(8,128)S(1)} %pad_maximum_fusion.21), channel_id=1, source_target_pairs={{8,0},{9,1},{10,2},{11,3},{12,4},{13,5},{14,6},{15,7},{16,8},{17,9... | collective-permute-start | bytes 1474568 | tf_op jit(solution)/shard_map/ppermute | solution.py:71
  335.1 13.3 %collective-permute-start.71 = (f32[2,3,5,32,128]{4,3,2,1,0:T(8,128)S(1)}, f32[2,3,5,32,128]{4,3,2,1,0:T(8,128)S(1)}, u32[]{:S(2)}, u32[]{:S(2)}) collective-permute-start(f32[2,3,5,32,128]{4,3,2,1,0:T(8,128)S(1)} %pad_maximum_fusion.21), channel_id=1, source_target_pairs={{16,0},{17,1},{18,2},{19,3},{20,4},{21,5},{22,6},{23,7},{24,8},{25... | collective-permute-start | bytes 1474568 | tf_op jit(solution)/shard_map/ppermute | solution.py:71
  336.4 24.7 %collective-permute-start.72 = (f32[2,3,5,32,128]{4,3,2,1,0:T(8,128)S(1)}, f32[2,3,5,32,128]{4,3,2,1,0:T(8,128)S(1)}, u32[]{:S(2)}, u32[]{:S(2)}) collective-permute-start(f32[2,3,5,32,128]{4,3,2,1,0:T(8,128)S(1)} %pad_maximum_fusion.21), channel_id=1, source_target_pairs={{24,0},{25,1},{26,2},{27,3},{28,4},{29,5},{30,6},{31,7},{0,8},{1,9... | collective-permute-start | bytes 1474568 | tf_op jit(solution)/shard_map/ppermute | solution.py:71
  (91 other events, 650.5 us)
